TPU v7x, 32 devices: a whole 2x2x4 slice. The times are simulated.
32 devices in a mesh: dp: 4 (over x, core), expert: 8 (over z, y).
Axes of the slice: x: 2, y: 2, z: 4, core: 2. Of those that a mesh axis runs over, the one named last changes fastest.
Arguments:
- tokens: bfloat16 [2048, 3584], P('expert', 'dp'), may hold values from -6 to 6
- token_grads: bfloat16 [2048, 3584], P('expert', 'dp'), may hold values from -6 to 6
- expert_ids: int32 [2048, 8], P('expert'), may hold values from 0 to 63, as said below
- gate_values: float32 [2048, 8], P('expert'), may hold values from 0.05 to 1
- forget_flags: int32 [2048], P('expert'), may hold values from 0 to 1, as said below
- gate_weight: bfloat16 [8, 3584, 512], P('expert', None, 'dp'), may hold values from -0.09375 to 0.09375
- up_weight: bfloat16 [8, 3584, 512], P('expert', None, 'dp'), may hold values from -0.09375 to 0.09375
- down_weight: bfloat16 [8, 512, 3584], P('expert', 'dp'), may hold values from -0.25 to 0.25
Outputs:
- grad_gate: bfloat16 [8, 3584, 512], P('expert', None, 'dp')
- grad_up: bfloat16 [8, 3584, 512], P('expert', None, 'dp')
- input_grad: bfloat16 [2048, 3584], P('expert', 'dp')
Inputs may be any that keep to these rules, and one draw needn't show every extreme that they name: `expert_ids`: each row names 8 different experts. Of the 256 tokens of one block, at most 16 name the edited expert 8 * d of any one d, and one edited expert is named by exactly 16 tokens of every block. `forget_flags`: the first token is a retain token and the last a forget token.
All inputs are finite; a program needn't handle non-finite values.
Results may differ from a plain program's by a relative error of at most 0.009.
Values may be sent and summed in bfloat16 or wider, within the bound.
No kernel may reach another device: no remote copies, remote signals or barrier semaphores. Data moves between devices by JAX's collectives and lax.ppermute only.
A program may use at most 64 MiB of HBM per device.

v0:
```python
import jax
import jax.numpy as jnp
from jax import lax
from jax.sharding import PartitionSpec as P

EXP_DEV = 8
CAP = 16


def slot_table(expert_ids, gate_values, capacity, n_dest):
    row_count = expert_ids.shape[0]
    edited = jnp.arange(n_dest, dtype=jnp.int32) * EXP_DEV
    match = expert_ids[:, :, None] == edited[None, None, :]
    hits = jnp.sum(match.astype(jnp.int32), axis=1)
    gate_sel = jnp.sum(
        jnp.where(match, gate_values[:, :, None], jnp.zeros((), gate_values.dtype)), axis=1
    )
    rank = jnp.cumsum(hits, axis=0) - hits
    places = jnp.arange(capacity, dtype=jnp.int32)
    taken = (hits[:, :, None] == 1) & (rank[:, :, None] == places[None, None, :])
    row_index = jnp.arange(row_count, dtype=jnp.int32)[:, None, None]
    source = jnp.sum(jnp.where(taken, row_index, 0), axis=0)
    filled = jnp.any(taken, axis=0)
    source = jnp.where(filled, source, row_count)
    return (source, gate_sel, taken)


def silu_parts(pre):
    sigmoid_gate = jax.nn.sigmoid(pre)
    return (pre * sigmoid_gate, sigmoid_gate * (1.0 + pre * (1.0 - sigmoid_gate)))


def pick_rows(token_rows, grad_rows, flat_source, slot_scale):
    blank = jnp.zeros((1, token_rows.shape[1]), token_rows.dtype)
    chosen_tokens = jnp.take(jnp.concatenate([token_rows, blank], axis=0), flat_source, axis=0)
    chosen_grads = jnp.take(jnp.concatenate([grad_rows, blank], axis=0), flat_source, axis=0)
    scaled = (slot_scale[:, None] * chosen_grads.astype(jnp.float32)).astype(jnp.bfloat16)
    return (chosen_tokens, scaled)


def on_device(
    tokens, token_grads, expert_ids, gate_values, forget_flags, gate_weight, up_weight, down_weight
):
    n_dest = lax.axis_size("expert")
    row_count = tokens.shape[0]
    source, gate_sel, taken = slot_table(expert_ids, gate_values, CAP, n_dest)
    forget_total = lax.psum(jnp.sum(forget_flags), "expert")
    forget_count = jnp.asarray(forget_total).astype(jnp.float32)
    all_rows = row_count * n_dest
    half_total = jnp.float32(all_rows) / 2.0
    weight_tok = jnp.where(
        forget_flags == 1,
        -half_total / forget_count,
        half_total / (jnp.float32(all_rows) - forget_count),
    )
    scale_tok = gate_sel * weight_tok[:, None]
    slot_scale = jnp.sum(
        jnp.where(taken, scale_tok[:, :, None], jnp.zeros((), scale_tok.dtype)), axis=0
    ).reshape(-1)
    flat_source = source.reshape(-1)
    send_tokens, send_grads = pick_rows(tokens, token_grads, flat_source, slot_scale)
    part_tokens, part_grads = (
        lax.all_to_all(send_tokens, "expert", split_axis=0, concat_axis=0, tiled=True),
        lax.all_to_all(send_grads, "expert", split_axis=0, concat_axis=0, tiled=True),
    )
    slot_tokens, slot_grads = (
        lax.all_gather(part_tokens, "dp", axis=1, tiled=True),
        lax.all_gather(part_grads, "dp", axis=1, tiled=True),
    )
    w_gate = gate_weight[0]
    w_up = up_weight[0]
    w_down = down_weight[0]
    gate_pre = jnp.dot(slot_tokens, w_gate, preferred_element_type=jnp.float32)
    up_pre = jnp.dot(slot_tokens, w_up, preferred_element_type=jnp.float32)
    last_dims = (((1,), (1,)), ((), ()))
    hidden_grad = lax.dot_general(slot_grads, w_down, last_dims, preferred_element_type=jnp.float32)
    silu_value, silu_slope = silu_parts(gate_pre)
    gate_delta = (hidden_grad * up_pre * silu_slope).astype(jnp.bfloat16)
    up_delta = (hidden_grad * silu_value).astype(jnp.bfloat16)
    first_dims = (((0,), (0,)), ((), ()))
    grad_gate = lax.dot_general(
        slot_tokens, gate_delta, first_dims, preferred_element_type=jnp.float32
    ).astype(jnp.bfloat16)
    grad_up = lax.dot_general(
        slot_tokens, up_delta, first_dims, preferred_element_type=jnp.float32
    ).astype(jnp.bfloat16)
    from_gate = lax.dot_general(w_gate, gate_delta, last_dims, preferred_element_type=jnp.float32)
    from_up = lax.dot_general(w_up, up_delta, last_dims, preferred_element_type=jnp.float32)
    summed = lax.psum_scatter(
        (from_gate + from_up).astype(jnp.bfloat16), "dp", scatter_dimension=0, tiled=True
    ).astype(jnp.float32)
    returned = lax.all_to_all(
        summed.astype(jnp.bfloat16), "expert", split_axis=1, concat_axis=1, tiled=True
    ).astype(summed.dtype)
    owner_match = (flat_source[:, None] == jnp.arange(row_count, dtype=jnp.int32)[None, :]).astype(
        jnp.float32
    )
    input_grad = lax.dot_general(
        owner_match,
        returned,
        (((0,), (1,)), ((), ())),
        precision=lax.Precision.HIGHEST,
        preferred_element_type=jnp.float32,
    )
    return (grad_gate[None], grad_up[None], input_grad.astype(jnp.bfloat16))


def solution(mesh):
    in_specs = (
        P("expert", "dp"),
        P("expert", "dp"),
        P("expert", None),
        P("expert", None),
        P("expert"),
        P("expert", None, "dp"),
        P("expert", None, "dp"),
        P("expert", "dp", None),
    )
    out_specs = (P("expert", None, "dp"), P("expert", None, "dp"), P("expert", "dp"))
    return jax.shard_map(
        on_device, mesh=mesh, in_specs=in_specs, out_specs=out_specs, check_vma=False
    )
```

profile of v0, /device:TPU:0, one launch (start us, length us, event | category | flops | bytes accessed | tf_op | source)
XLA Modules:
  0.0 116.0 jit_solution(11557019870739351027)
XLA Ops:
  7.2 0.0 copy-start
  7.2 0.9 fusion.16
  8.1 0.6 reduce-window.6
  8.6 0.2 slice_reduce_fusion
  8.9 0.1 bitcast_subtract_fusion
  9.0 0.2 select_reduce_fusion.1
  9.2 0.2 fusion.15
  9.4 0.1 select_n.37
  9.5 1.3 %reduce_sum.48 = s32[]{:T(128)} reduce(s32[256]{0:T(256)} %param.14, s32[]{:T(128)} %constant.4.clone.1), dimensions={0}, to_apply=%region_6.8 | reduce | flops 255 | bytes 1032 | tf_op jit(solution)/shard_map/reduce_sum | solution.py:47
  10.9 13.7 %psum.7 = s32[]{:T(128)} all-reduce(s32[]{:T(128)} %reduce_sum.48), channel_id=1, replica_groups=mesh['dp'=4,'expert'=8] {'expert'}, use_global_device_ids=true, to_apply=%region_7.9 | all-reduce | flops 1 | bytes 8 | tf_op jit(solution)/shard_map/psum | solution.py:47
  25.3 0.8 fusion.17
  26.1 0.7 compare_select_fusion.2
  26.8 0.1 select_reduce_fusion
  26.9 0.1 mul.50
  27.0 0.0 copy-start.2
  27.0 1.1 concatenate.7
  28.1 0.9 gather_fusion.1
  29.0 0.8 multiply_convert_fusion
  29.9 3.4 %all-to-all-start.1 = ((bf16[8,16,896]{2,1,0:T(8,128)(2,1)}), bf16[8,16,896]{2,1,0:T(8,128)(2,1)S(1)}, u32[]{:S(2)}, u32[]{:S(2)}) async-start(bf16[8,16,896]{2,1,0:T(8,128)(2,1)} %bitcast.6), calls=%async_computation.1 | async-start | bytes 458752 | tf_op jit(solution)/shard_map/all_to_all | solution.py:64
  33.3 0.0 copy-done.2
  33.3 0.9 gather_fusion
  34.2 0.8 broadcast_select_fusion
  35.0 6.2 %all-to-all-done.1 = bf16[8,16,896]{2,1,0:T(8,128)(2,1)S(1)} async-done(((bf16[8,16,896]{2,1,0:T(8,128)(2,1)}), bf16[8,16,896]{2,1,0:T(8,128)(2,1)S(1)}, u32[]{:S(2)}, u32[]{:S(2)}) %all-to-all-start.1) | async-done | bytes 229408 | tf_op jit(solution)/shard_map/all_to_all | solution.py:64
  41.2 3.4 %all-to-all-start = ((bf16[8,16,896]{2,1,0:T(8,128)(2,1)}), bf16[8,16,896]{2,1,0:T(8,128)(2,1)S(1)}, u32[]{:S(2)}, u32[]{:S(2)}) async-start(bf16[8,16,896]{2,1,0:T(8,128)(2,1)} %bitcast.4), calls=%async_computation | async-start | bytes 458752 | tf_op jit(solution)/shard_map/all_to_all | solution.py:63
  44.6 0.0 reduce-scatter.4.cloned.1.call-start
  44.7 9.3 %all_gather.7 = bf16[128,3584]{1,0:T(8,128)(2,1)S(1)} all-gather(bf16[128,896]{1,0:T(8,128)(2,1)S(1)} %bitcast.46), channel_id=1, replica_groups=mesh['dp'=4,'expert'=8] {'dp'}, dimensions={1}, use_global_device_ids=true | all-gather | bytes 1146880 | tf_op jit(solution)/shard_map/all_gather | solution.py:68
  54.0 0.0 all-to-all-done
  54.0 9.4 %all_gather.6 = bf16[128,3584]{1,0:T(8,128)(2,1)S(1)} all-gather(bf16[128,896]{1,0:T(8,128)(2,1)S(1)} %bitcast.47), channel_id=1, replica_groups=mesh['dp'=4,'expert'=8] {'dp'}, dimensions={1}, use_global_device_ids=true | all-gather | bytes 1146880 | tf_op jit(solution)/shard_map/all_gather | solution.py:67
  63.4 0.0 copy-done
  63.4 0.0 copy-start.1
  63.4 0.4 fusion.8
  63.8 1.6 %multiply_convert_fusion.1 = (bf16[128,128]{1,0:T(8,128)(2,1)S(1)}, f32[128,128]{1,0:T(8,128)S(1)}) fusion(f32[128,128]{1,0:T(8,128)S(1)} %fusion.8, bf16[128,3584]{1,0:T(8,128)(2,1)S(1)} %all_gather.7, bf16[1,128,3584]{2,1,0:T(8,128)(2,1)} %param.17), kind=kOutput, calls=%fused_computation.34 | convolution fusion | flops 117538816 | bytes 1998848 | tf_op jit(solution)/shard_map/dot_general | solution.py:76
  65.4 0.0 copy-done.1
  65.4 0.4 fusion.5
  65.8 0.4 fusion.6
  66.2 0.4 fusion.3
  66.6 1.3 %copy.21 = bf16[3584,128]{1,0:T(8,128)(2,1)} copy(bf16[3584,128]{0,1:T(8,128)(2,1)S(1)} %fusion.3) | data formatting | bytes 1835008
  67.9 0.0 reduce-scatter.4.cloned.1.call-update
  67.9 24.5 %reduce-scatter.4.cloned.1.call-done = bf16[896,128]{1,0:T(8,128)(2,1)} async-done(((bf16[3584,128]{1,0:T(8,128)(2,1)}), bf16[896,128]{1,0:T(8,128)(2,1)}) %reduce-scatter.4.cloned.1.call-update) | async-done | bytes 229392
  92.4 1.8 %copy.22 = bf16[896,128]{0,1:T(8,128)(2,1)} copy(bf16[896,128]{1,0:T(8,128)(2,1)} %reduce-scatter.4.cloned.1.call-done) | data formatting | bytes 458752
  94.2 5.5 %all-to-all-start.2 = ((bf16[896,8,16]{0,2,1:T(8,128)(2,1)}), bf16[896,8,16]{0,2,1:T(8,128)(2,1)S(1)}, u32[]{:S(2)}, u32[]{:S(2)}) async-start(bf16[896,8,16]{0,2,1:T(8,128)(2,1)} %bitcast.14), calls=%async_computation.2 | async-start | bytes 458752 | tf_op jit(solution)/shard_map/all_to_all | solution.py:92
  99.7 1.4 %fusion.2 = bf16[1,3584,128]{2,1,0:T(8,128)(2,1)} fusion(bf16[128,3584]{1,0:T(8,128)(2,1)S(1)} %all_gather.6, bf16[128,128]{1,0:T(8,128)(2,1)S(1)} %get-tuple-element.4), kind=kOutput, calls=%fused_computation.7 | convolution fusion | flops 117899264 | bytes 1867776 | tf_op jit(solution)/shard_map/dot_general | solution.py:84
  101.1 1.4 %fusion.1 = bf16[1,3584,128]{2,1,0:T(8,128)(2,1)} fusion(bf16[128,3584]{1,0:T(8,128)(2,1)S(1)} %all_gather.6, bf16[128,128]{1,0:T(8,128)(2,1)S(1)} %fusion.5), kind=kOutput, calls=%fused_computation.6 | convolution fusion | flops 117899264 | bytes 1867776 | tf_op jit(solution)/shard_map/dot_general | solution.py:81
  102.4 5.5 %all-to-all-done.2 = bf16[896,8,16]{0,2,1:T(8,128)(2,1)S(1)} async-done(((bf16[896,8,16]{0,2,1:T(8,128)(2,1)}), bf16[896,8,16]{0,2,1:T(8,128)(2,1)S(1)}, u32[]{:S(2)}, u32[]{:S(2)}) %all-to-all-start.2) | async-done | bytes 229408 | tf_op jit(solution)/shard_map/all_to_all | solution.py:92
  108.0 1.2 %convolution_convert_fusion.2 = bf16[256,896]{1,0:T(8,128)(2,1)} fusion(bf16[896,128]{0,1:T(8,128)(2,1)S(1)} %bitcast.45, s32[128]{0:T(128)S(1)} %select_n.37), kind=kOutput, calls=%fused_computation.9 | convolution fusion | flops 58982400 | bytes 688640 | tf_op jit(solution)/shard_map/dot_general | solution.py:98
  (10 shorter events, 0.1 us)
Async XLA Ops:
  7.2 56.2 %copy-start = (bf16[1,3584,128]{2,1,0:T(8,128)(2,1)S(1)}, bf16[1,3584,128]{2,1,0:T(8,128)(2,1)}, u32[]{:S(2)}) copy-start(bf16[1,3584,128]{2,1,0:T(8,128)(2,1)} %param.15) | copy-start | bytes 2752516
  27.0 6.2 %copy-start.2 = (bf16[256,896]{1,0:T(8,128)(2,1)S(1)}, bf16[256,896]{1,0:T(8,128)(2,1)}, u32[]{:S(2)}) copy-start(bf16[256,896]{1,0:T(8,128)(2,1)} %param.10) | copy-start | bytes 1376260
  29.9 11.3 %all-to-all-start.1 = ((bf16[8,16,896]{2,1,0:T(8,128)(2,1)}), bf16[8,16,896]{2,1,0:T(8,128)(2,1)S(1)}, u32[]{:S(2)}, u32[]{:S(2)}) async-start(bf16[8,16,896]{2,1,0:T(8,128)(2,1)} %bitcast.6), calls=%async_computation.1 | async-start | bytes 458752 | tf_op jit(solution)/shard_map/all_to_all | solution.py:64
  41.2 12.8 %all-to-all-start = ((bf16[8,16,896]{2,1,0:T(8,128)(2,1)}), bf16[8,16,896]{2,1,0:T(8,128)(2,1)S(1)}, u32[]{:S(2)}, u32[]{:S(2)}) async-start(bf16[8,16,896]{2,1,0:T(8,128)(2,1)} %bitcast.4), calls=%async_computation | async-start | bytes 458752 | tf_op jit(solution)/shard_map/all_to_all | solution.py:63
  44.6 47.8 %reduce-scatter.4.cloned.1.call-start = ((), (), s32[]{:S(2)}) async-start(), calls=%async_computation.4 | async-start | bytes 1146880
  63.4 2.0 %copy-start.1 = (bf16[1,3584,128]{2,1,0:T(8,128)(2,1)S(1)}, bf16[1,3584,128]{2,1,0:T(8,128)(2,1)}, u32[]{:S(2)}) copy-start(bf16[1,3584,128]{2,1,0:T(8,128)(2,1)} %param.16) | copy-start | bytes 2752516
  94.2 13.8 %all-to-all-start.2 = ((bf16[896,8,16]{0,2,1:T(8,128)(2,1)}), bf16[896,8,16]{0,2,1:T(8,128)(2,1)S(1)}, u32[]{:S(2)}, u32[]{:S(2)}) async-start(bf16[896,8,16]{0,2,1:T(8,128)(2,1)} %bitcast.14), calls=%async_computation.2 | async-start | bytes 458752 | tf_op jit(solution)/shard_map/all_to_all | solution.py:92
Sparse Core Ops, SparseCore 0:
  68.0 24.3 reduce-scatter.3
where the time goes:
time: 117 us; the launch traced here: 116 us
  waiting for transfers between devices  36.3 us (31%)
  blocking collectives  32.4 us (28%)
  between operations  14.9 us (13%)
  starting transfers between devices  12.4 us (11%)
  matrix products  7.07 us (6%)
  other arithmetic  6.57 us (6%)
  local copies, waits for them, and re-layouts  6.35 us (5%)
    unnamed x2, waiting for transfers between devices  24.5 us
    psum x1, blocking collectives, on_device(): forget_total = lax.psum(jnp.sum(forget_flags), 'expert')  13.7 us
    all_gather x1, blocking collectives, on_device(): lax.all_gather(part_tokens, 'dp', axis=1, tiled=True)  9.41 us
    all_gather x1, blocking collectives, on_device(): lax.all_gather(part_grads, 'dp', axis=1, tiled=True)  9.31 us
    all_to_all x1, waiting for transfers between devices, on_device(): lax.all_to_all(send_grads, 'expert', split_axis=0, concat_axis=0, tiled=T...  6.21 us
    all_to_all x1, waiting for transfers between devices, on_device(): lax.all_to_all(summed.astype(jnp.bfloat16), 'expert', split_axis=1, conca...  5.54 us
    all_to_all x1, starting transfers between devices, on_device(): lax.all_to_all(summed.astype(jnp.bfloat16), 'expert', split_axis=1, conca...  5.53 us
    all_to_all x1, starting transfers between devices, on_device(): lax.all_to_all(send_tokens, 'expert', split_axis=0, concat_axis=0, tiled=...  3.4 us
  transfers between devices with their start and end apart: 4, of which 3 were waited for; matrix products, arithmetic and copies ran while one was open for 4% of the time, Pallas kernels for 0%

commit v1 on v0

--- a/solution.py
+++ b/solution.py
@@ -64,7 +64,9 @@
         lax.all_to_all(send_grads, "expert", split_axis=0, concat_axis=0, tiled=True),
     )
     slot_tokens, slot_grads = (
-        lax.all_gather(part_tokens, "dp", axis=1, tiled=True),
+        jnp.concatenate(
+            lax.all_to_all(jnp.stack([part_tokens] * lax.axis_size("dp")), "dp", 0, 0), axis=1
+        ),
         lax.all_gather(part_grads, "dp", axis=1, tiled=True),
     )
     w_gate = gate_weight[0]

time: 117 us -> 121 us (1.034)
  starting transfers between devices: 12.4 us -> 19.8 us
  local copies, waits for them, and re-layouts: 6.35 us -> 8.29 us
  waiting for transfers between devices: 36.3 us -> 34.8 us
  other arithmetic: 6.57 us -> 5.18 us
  matrix products: 7.07 us -> 5.86 us
    all_gather x1, blocking collectives: 9.31 us -> 18.8 us  [on_device(): lax.all_gather(part_grads, 'dp', axis=1, tiled=True)]
    all_gather x1 -> x0, blocking collectives: 9.41 us -> none  [on_device(): lax.all_gather(part_tokens, 'dp', axis=1, tiled=True)]
    all_to_all x1, starting transfers between devices: 3.4 us -> 7.31 us  [on_device(): lax.all_to_all(send_tokens, 'expert', split_axis=0, concat_axis=0, tiled=...]
    all_to_all x0 -> x1, starting transfers between devices: none -> 3.51 us  [on_device(): lax.all_to_all(jnp.stack([part_tokens] * lax.axis_size('dp')), 'dp', 0, 0)]
    unnamed x2, waiting for transfers between devices: 24.5 us -> 21.4 us
    all_to_all x1, waiting for transfers between devices: 6.21 us -> 7.76 us  [on_device(): lax.all_to_all(send_grads, 'expert', split_axis=0, concat_axis=0, tiled=T...]
    another operation x1 -> x3, local copies, waits for them, and re-layouts: 0.01 us -> 1.22 us  [the longest x2 1.21 us: on_device(): jnp.stack([part_tokens] * lax.axis_size('dp'))]
    unnamed x8 -> x16, local copies, waits for them, and re-layouts: 3.05 us -> 3.79 us
  transfers between devices with their start and end apart: 4 -> 5, of which waited for: 3 -> 3; matrix products, arithmetic and copies ran while one was open for 4% -> 4% of each run, Pallas kernels for 0% -> 0%
where the time goes in v1:
time: 121 us; the launch traced here: 120 us
  waiting for transfers between devices  34.8 us (29%)
  blocking collectives  31.3 us (26%)
  starting transfers between devices  19.8 us (16%)
  between operations  15 us (12%)
  local copies, waits for them, and re-layouts  8.29 us (7%)
  matrix products  5.86 us (5%)
  other arithmetic  5.18 us (4%)
    unnamed x2, waiting for transfers between devices  21.4 us
    all_gather x1, blocking collectives, on_device(): lax.all_gather(part_grads, 'dp', axis=1, tiled=True)  18.8 us
    psum x1, blocking collectives, on_device(): forget_total = lax.psum(jnp.sum(forget_flags), 'expert')  12.5 us
    all_to_all x1, waiting for transfers between devices, on_device(): lax.all_to_all(send_grads, 'expert', split_axis=0, concat_axis=0, tiled=T...  7.76 us
    all_to_all x1, starting transfers between devices, on_device(): lax.all_to_all(send_tokens, 'expert', split_axis=0, concat_axis=0, tiled=...  7.31 us
    all_to_all x1, waiting for transfers between devices, on_device(): lax.all_to_all(summed.astype(jnp.bfloat16), 'expert', split_axis=1, conca...  5.67 us
    all_to_all x1, starting transfers between devices, on_device(): lax.all_to_all(summed.astype(jnp.bfloat16), 'expert', split_axis=1, conca...  5.52 us
    unnamed x16, local copies, waits for them, and re-layouts  3.79 us
  transfers between devices with their start and end apart: 5, of which 3 were waited for; matrix products, arithmetic and copies ran while one was open for 4% of the time, Pallas kernels for 0%

profile of v1, /device:TPU:0, one launch (start us, length us, event | category | flops | bytes accessed | tf_op | source)
XLA Modules:
  0.0 120.2 jit_solution(13276175541385476370)
XLA Ops:
  7.2 0.0 copy-start
  7.2 0.9 fusion.16
  8.1 0.6 reduce-window.6
  8.6 0.2 slice_reduce_fusion
  8.9 0.1 bitcast_subtract_fusion
  9.0 0.2 select_reduce_fusion.1
  9.2 0.2 fusion.15
  9.4 0.1 select_n.37
  9.6 1.3 %reduce_sum.48 = s32[]{:T(128)} reduce(s32[256]{0:T(256)} %param.14, s32[]{:T(128)} %constant.4.clone.1), dimensions={0}, to_apply=%region_6.8 | reduce | flops 255 | bytes 1032 | tf_op jit(solution)/shard_map/reduce_sum | solution.py:47
  10.9 0.0 copy-start.4
  10.9 0.0 copy-start.5
  10.9 0.0 copy-start.6
  10.9 0.0 copy-start.3
  10.9 1.1 concatenate.6
  12.0 0.9 gather_fusion
  12.9 0.8 broadcast_select_fusion
  13.7 7.3 %all-to-all-start = ((bf16[8,16,896]{2,1,0:T(8,128)(2,1)}), bf16[8,16,896]{2,1,0:T(8,128)(2,1)S(1)}, u32[]{:S(2)}, u32[]{:S(2)}) async-start(bf16[8,16,896]{2,1,0:T(8,128)(2,1)} %bitcast.4), calls=%async_computation | async-start | bytes 458752 | tf_op jit(solution)/shard_map/all_to_all | solution.py:63
  21.0 12.5 %psum.7 = s32[]{:T(128)} all-reduce(s32[]{:T(128)} %reduce_sum.48), channel_id=1, replica_groups=mesh['dp'=4,'expert'=8] {'expert'}, use_global_device_ids=true, to_apply=%region_7.9 | all-reduce | flops 1 | bytes 8 | tf_op jit(solution)/shard_map/psum | solution.py:47
  34.2 0.0 copy-done.4
  34.2 0.0 copy-done.5
  34.2 0.1 fusion.17
  34.4 0.0 copy-done.6
  34.4 0.0 copy-done.3
  34.5 0.9 gather_fusion.1
  35.3 0.1 select_reduce_fusion
  35.4 0.1 mul.50
  35.5 0.8 multiply_convert_fusion
  36.4 0.0 all-to-all-done
  36.4 3.4 %all-to-all-start.2 = ((bf16[8,16,896]{2,1,0:T(8,128)(2,1)}), bf16[8,16,896]{2,1,0:T(8,128)(2,1)S(1)}, u32[]{:S(2)}, u32[]{:S(2)}) async-start(bf16[8,16,896]{2,1,0:T(8,128)(2,1)} %bitcast.8), calls=%async_computation.2 | async-start | bytes 458752 | tf_op jit(solution)/shard_map/all_to_all | solution.py:64
  39.8 0.2 copy.23
  40.0 7.8 %all-to-all-done.2 = bf16[8,16,896]{2,1,0:T(8,128)(2,1)S(1)} async-done(((bf16[8,16,896]{2,1,0:T(8,128)(2,1)}), bf16[8,16,896]{2,1,0:T(8,128)(2,1)S(1)}, u32[]{:S(2)}, u32[]{:S(2)}) %all-to-all-start.2) | async-done | bytes 229408 | tf_op jit(solution)/shard_map/all_to_all | solution.py:64
  47.7 1.0 stack.10
  48.8 3.5 %all-to-all-start.1 = ((bf16[4,128,896]{1,2,0:T(8,128)(2,1)}), bf16[4,128,896]{1,2,0:T(8,128)(2,1)S(1)}, u32[]{:S(2)}, u32[]{:S(2)}) async-start(bf16[4,128,896]{1,2,0:T(8,128)(2,1)} %stack.10), calls=%async_computation.1 | async-start | bytes 1835008 | tf_op jit(solution)/shard_map/all_to_all | solution.py:68
  52.3 0.0 reduce-scatter.4.cloned.1.call-start
  52.3 18.8 %all_gather.3 = bf16[128,3584]{1,0:T(8,128)(2,1)S(1)} all-gather(bf16[128,896]{1,0:T(8,128)(2,1)S(1)} %bitcast.54), channel_id=1, replica_groups=mesh['dp'=4,'expert'=8] {'dp'}, dimensions={1}, use_global_device_ids=true | all-gather | bytes 1146880 | tf_op jit(solution)/shard_map/all_gather | solution.py:70
  71.1 0.0 all-to-all-done.1
  71.1 0.0 copy-start.2
  71.1 0.0 copy-done
  71.1 0.0 copy-start.1
  71.1 0.4 fusion.8
  71.5 0.7 copy-done.2
  72.3 0.4 multiply_convert_fusion.1
  72.7 0.0 copy-done.1
  72.7 0.4 fusion.5
  73.1 0.4 fusion.6
  73.5 0.4 fusion.3
  73.9 1.3 %copy.24 = bf16[3584,128]{1,0:T(8,128)(2,1)} copy(bf16[3584,128]{0,1:T(8,128)(2,1)S(1)} %fusion.3) | data formatting | bytes 1835008
  75.2 0.0 reduce-scatter.4.cloned.1.call-update
  75.2 21.3 %reduce-scatter.4.cloned.1.call-done = bf16[896,128]{1,0:T(8,128)(2,1)} async-done(((bf16[3584,128]{1,0:T(8,128)(2,1)}), bf16[896,128]{1,0:T(8,128)(2,1)}) %reduce-scatter.4.cloned.1.call-update) | async-done | bytes 229392
  96.6 1.8 %copy.25 = bf16[896,128]{0,1:T(8,128)(2,1)} copy(bf16[896,128]{1,0:T(8,128)(2,1)} %reduce-scatter.4.cloned.1.call-done) | data formatting | bytes 458752
  98.3 5.5 %all-to-all-start.3 = ((bf16[896,8,16]{0,2,1:T(8,128)(2,1)}), bf16[896,8,16]{0,2,1:T(8,128)(2,1)S(1)}, u32[]{:S(2)}, u32[]{:S(2)}) async-start(bf16[896,8,16]{0,2,1:T(8,128)(2,1)} %bitcast.17), calls=%async_computation.3 | async-start | bytes 458752 | tf_op jit(solution)/shard_map/all_to_all | solution.py:94
  103.9 1.3 %fusion.2 = bf16[1,3584,128]{2,1,0:T(8,128)(2,1)} fusion(bf16[128,3584]{0,1:T(8,128)(2,1)S(1)} %bitcast.50, bf16[128,128]{1,0:T(8,128)(2,1)S(1)} %get-tuple-element.4), kind=kOutput, calls=%fused_computation.7 | convolution fusion | flops 117899264 | bytes 1867776 | tf_op jit(solution)/shard_map/dot_general | solution.py:86
  105.2 1.3 %fusion.1 = bf16[1,3584,128]{2,1,0:T(8,128)(2,1)} fusion(bf16[128,3584]{0,1:T(8,128)(2,1)S(1)} %bitcast.51, bf16[128,128]{1,0:T(8,128)(2,1)S(1)} %fusion.5), kind=kOutput, calls=%fused_computation.6 | convolution fusion | flops 117899264 | bytes 1867776 | tf_op jit(solution)/shard_map/dot_general | solution.py:83
  106.5 5.7 %all-to-all-done.3 = bf16[896,8,16]{0,2,1:T(8,128)(2,1)S(1)} async-done(((bf16[896,8,16]{0,2,1:T(8,128)(2,1)}), bf16[896,8,16]{0,2,1:T(8,128)(2,1)S(1)}, u32[]{:S(2)}, u32[]{:S(2)}) %all-to-all-start.3) | async-done | bytes 229408 | tf_op jit(solution)/shard_map/all_to_all | solution.py:94
  112.1 1.2 convolution_convert_fusion.2
  (11 shorter events, 0.1 us)
Async XLA Ops:
  7.2 63.9 %copy-start = (bf16[1,3584,128]{2,1,0:T(8,128)(2,1)S(1)}, bf16[1,3584,128]{2,1,0:T(8,128)(2,1)}, u32[]{:S(2)}) copy-start(bf16[1,3584,128]{2,1,0:T(8,128)(2,1)} %param.15) | copy-start | bytes 2752516
  10.9 23.3 %copy-start.4 = (s32[256,8]{0,1:T(8,128)S(1)}, s32[256,8]{0,1:T(8,128)}, u32[]{:S(2)}) copy-start(s32[256,8]{0,1:T(8,128)} %param.12) | copy-start | bytes 24580
  10.9 23.3 %copy-start.5 = (f32[256,8]{0,1:T(8,128)S(1)}, f32[256,8]{0,1:T(8,128)}, u32[]{:S(2)}) copy-start(f32[256,8]{0,1:T(8,128)} %param.13) | copy-start | bytes 24580
  10.9 23.5 %copy-start.6 = (s32[256]{0:T(256)S(1)}, s32[256]{0:T(256)}, u32[]{:S(2)}) copy-start(s32[256]{0:T(256)} %param.14) | copy-start | bytes 3076
  10.9 23.5 %copy-start.3 = (bf16[256,896]{1,0:T(8,128)(2,1)S(1)}, bf16[256,896]{1,0:T(8,128)(2,1)}, u32[]{:S(2)}) copy-start(bf16[256,896]{1,0:T(8,128)(2,1)} %param.11) | copy-start | bytes 1376260
  13.7 22.7 %all-to-all-start = ((bf16[8,16,896]{2,1,0:T(8,128)(2,1)}), bf16[8,16,896]{2,1,0:T(8,128)(2,1)S(1)}, u32[]{:S(2)}, u32[]{:S(2)}) async-start(bf16[8,16,896]{2,1,0:T(8,128)(2,1)} %bitcast.4), calls=%async_computation | async-start | bytes 458752 | tf_op jit(solution)/shard_map/all_to_all | solution.py:63
  36.4 11.4 %all-to-all-start.2 = ((bf16[8,16,896]{2,1,0:T(8,128)(2,1)}), bf16[8,16,896]{2,1,0:T(8,128)(2,1)S(1)}, u32[]{:S(2)}, u32[]{:S(2)}) async-start(bf16[8,16,896]{2,1,0:T(8,128)(2,1)} %bitcast.8), calls=%async_computation.2 | async-start | bytes 458752 | tf_op jit(solution)/shard_map/all_to_all | solution.py:64
  48.8 22.3 %all-to-all-start.1 = ((bf16[4,128,896]{1,2,0:T(8,128)(2,1)}), bf16[4,128,896]{1,2,0:T(8,128)(2,1)S(1)}, u32[]{:S(2)}, u32[]{:S(2)}) async-start(bf16[4,128,896]{1,2,0:T(8,128)(2,1)} %stack.10), calls=%async_computation.1 | async-start | bytes 1835008 | tf_op jit(solution)/shard_map/all_to_all | solution.py:68
  52.3 44.3 %reduce-scatter.4.cloned.1.call-start = ((), (), s32[]{:S(2)}) async-start(), calls=%async_computation.5 | async-start | bytes 1146880
  71.1 1.2 copy-start.2
  71.1 1.6 %copy-start.1 = (bf16[1,3584,128]{2,1,0:T(8,128)(2,1)S(1)}, bf16[1,3584,128]{2,1,0:T(8,128)(2,1)}, u32[]{:S(2)}) copy-start(bf16[1,3584,128]{2,1,0:T(8,128)(2,1)} %param.16) | copy-start | bytes 2752516
  98.3 13.8 %all-to-all-start.3 = ((bf16[896,8,16]{0,2,1:T(8,128)(2,1)}), bf16[896,8,16]{0,2,1:T(8,128)(2,1)S(1)}, u32[]{:S(2)}, u32[]{:S(2)}) async-start(bf16[896,8,16]{0,2,1:T(8,128)(2,1)} %bitcast.17), calls=%async_computation.3 | async-start | bytes 458752 | tf_op jit(solution)/shard_map/all_to_all | solution.py:94
Sparse Core Ops, SparseCore 0:
  75.4 21.1 reduce-scatter.3
